TPU v7x, 32 devices: a whole 2x2x4 slice. The times are simulated.
32 devices in a mesh: grp: 2 (over x), blk: 16 (over z, y, core).
Axes of the slice: x: 2, y: 2, z: 4, core: 2. Of those that a mesh axis runs over, the one named last changes fastest.
Arguments:
- tokens: bfloat16 [16384, 1024], P(('grp', 'blk')), parts along dimension 0, may hold values from -6 to 6
- patch_of_row: int32 [16384], P(('grp', 'blk')), parts along dimension 0, may hold values from 0 to 2047, as said below
- latents: bfloat16 [256, 1024], P('blk'), may hold values from -110 to 110
- contrast_gain: bfloat16 [4, 1024], replicated, may hold values from 0.099609375 to 1.8984375
- norm_gain: bfloat16 [1024], replicated, may hold values from 0.099609375 to 1.8984375
- w_query: bfloat16 [1024, 1024], replicated, may hold values from -0.1875 to 0.1875
- w_key: bfloat16 [1024, 1024], replicated, may hold values from -0.1875 to 0.1875
- w_value: bfloat16 [1024, 1024], replicated, may hold values from -0.1875 to 0.1875
- w_out: bfloat16 [1024, 1024], replicated, may hold values from -0.1875 to 0.1875
Outputs:
- new_latents: bfloat16 [512, 1024], P(('grp', 'blk')), parts along dimension 0
There are 2 independent parts, one for each index of `grp`. A program takes and returns all parts, laid end to end along the dimension named above; an argument that names none is the same for every part. Nothing has to cross between parts.
Inputs may be any that keep to these rules, and one draw needn't show every extreme that they name: `patch_of_row`: for each contrast c, rows c * 2048 to (c + 1) * 2048 - 1 name every patch once, and row c * 2048 + s names a patch p with p // 128 == s % 16.
All inputs are finite; a program needn't handle non-finite values.
Results may differ from a plain program's by a relative error of at most 0.0065.
Values may be sent and summed in bfloat16 or wider, within the bound.
No kernel may reach another device: no remote copies, remote signals or barrier semaphores. Data moves between devices by JAX's collectives and lax.ppermute only.
A program may use at most 64 MiB of HBM per device.

v0:
```python
import jax
import jax.numpy as jnp
from jax import lax
from jax.sharding import PartitionSpec as P

HEADS = 16
CONTRASTS = 4


def shifted(block, axis, distance):
    devices = range(lax.axis_size(axis))
    route = [((i - distance) % len(devices), i) for i in devices]
    return lax.ppermute(block, axis, route)


def absorb(tile, maxima, totals, accum, key_heads, value_heads):
    tile_rows, model_width = tile.shape
    head_count, head_width = (key_heads.shape[1], key_heads.shape[2])
    tile_heads = tile.reshape(tile_rows, head_count, head_width)
    scores = jnp.einsum("lhd,khd->lhk", tile_heads, key_heads, preferred_element_type=jnp.float32)
    raised = jnp.maximum(maxima, jnp.max(scores, axis=-1))
    factor = jnp.exp(maxima - raised)
    weights = jnp.exp(scores - raised[..., None])
    totals = totals * factor + jnp.sum(weights, axis=-1)
    summed = jnp.einsum(
        "lhk,khd->lhd",
        weights.astype(jnp.bfloat16),
        value_heads,
        preferred_element_type=jnp.float32,
    )
    accum = accum.reshape(tile_rows, head_count, head_width) * factor[..., None] + summed
    return (raised, totals, accum.reshape(tile_rows, model_width))


def fresh_state(tile_rows, head_count, model_width):
    return (
        jnp.full((tile_rows, head_count), -1e30, jnp.float32),
        jnp.zeros((tile_rows, head_count), jnp.float32),
        jnp.zeros((tile_rows, model_width), jnp.float32),
    )


def pass_one(state):
    return (
        shifted(state[0].astype(jnp.bfloat16), "blk", 1).astype(jnp.float32),
        shifted(state[1].astype(jnp.bfloat16), "blk", 1).astype(jnp.float32),
        shifted(state[2].astype(jnp.bfloat16), "blk", 1).astype(jnp.float32),
    )


def local(tokens, patch_of_row, latents, contrast_gain, norm_gain, w_query, w_key, w_value, w_out):
    cycle_size = lax.axis_size("blk")
    my_index = lax.axis_index("blk")
    tok_rows, model_width = tokens.shape
    head_count = HEADS
    head_width = model_width // head_count
    per_peer = tok_rows // cycle_size
    patches_dev = tok_rows // CONTRASTS
    received = lax.all_to_all(
        tokens.reshape(per_peer, cycle_size, model_width),
        "blk",
        split_axis=1,
        concat_axis=1,
        tiled=True,
    )
    received_ids = lax.all_to_all(
        patch_of_row.reshape(per_peer, cycle_size), "blk", split_axis=1, concat_axis=1, tiled=True
    )
    source_dev = lax.broadcasted_iota(jnp.int32, (per_peer, cycle_size), 1)
    row_step = lax.broadcasted_iota(jnp.int32, (per_peer, cycle_size), 0)
    slot_index = source_dev * tok_rows + my_index + cycle_size * row_step
    contrast_id = slot_index // (patches_dev * cycle_size)
    target_row = (contrast_id * patches_dev + received_ids - my_index * patches_dev).reshape(
        tok_rows
    )
    inverse = (
        jnp.zeros((tok_rows,), jnp.int32).at[target_row].set(jnp.arange(tok_rows, dtype=jnp.int32))
    )
    arranged = received.reshape(tok_rows, model_width)[inverse].reshape(
        CONTRASTS, patches_dev, model_width
    )
    joined = jnp.sum(
        arranged.astype(jnp.float32) * contrast_gain.astype(jnp.float32)[:, None, :], axis=0
    )
    inverse_rms = lax.rsqrt(jnp.mean(joined * joined, axis=-1, keepdims=True) + 1e-05)
    normed = (joined * inverse_rms * norm_gain.astype(jnp.float32)).astype(jnp.bfloat16)
    key_rows = jnp.dot(normed, w_key, preferred_element_type=jnp.float32).astype(jnp.bfloat16)
    value_rows = jnp.dot(normed, w_value, preferred_element_type=jnp.float32).astype(jnp.bfloat16)
    key_heads = key_rows.reshape(patches_dev, head_count, head_width)
    value_heads = value_rows.reshape(patches_dev, head_count, head_width)
    queries = (
        jnp.dot(latents, w_query, preferred_element_type=jnp.float32) * head_width ** (-0.5)
    ).astype(jnp.bfloat16)
    lat_rows = latents.shape[0]

    def hop_step(index_hop, state_carry):
        tile, maxima, totals, accum = state_carry
        state = absorb(tile, maxima, totals, accum, key_heads, value_heads)
        tile = shifted(tile, "blk", 1)
        maxima, totals, accum = pass_one(state)
        return (tile, maxima, totals, accum)

    begin = (queries,) + fresh_state(lat_rows, head_count, model_width)
    tile, maxima, totals, accum = lax.fori_loop(0, cycle_size - 1, hop_step, begin)
    maxima, totals, accum = pass_one(absorb(tile, maxima, totals, accum, key_heads, value_heads))
    attended = (
        (accum.reshape(lat_rows, head_count, head_width) / totals[..., None])
        .reshape(lat_rows, model_width)
        .astype(jnp.bfloat16)
    )
    mixed = latents.astype(jnp.float32) + jnp.dot(
        attended, w_out, preferred_element_type=jnp.float32
    )
    return mixed.astype(jnp.bfloat16)


def solution(mesh):
    in_specs = (
        P(("grp", "blk"), None),
        P(("grp", "blk")),
        P("blk", None),
        P(),
        P(),
        P(),
        P(),
        P(),
        P(),
    )
    out_specs = P(("grp", "blk"), None)
    return jax.shard_map(local, mesh=mesh, in_specs=in_specs, out_specs=out_specs, check_vma=False)
```

profile of v0, /device:TPU:0, one launch (start us, length us, event | category | flops | bytes accessed | tf_op | source)
XLA Modules:
  0.0 180.4 jit_solution(3693052724654784124)
XLA Ops:
  1.6 7.4 %all-to-all-start.1 = ((s32[32,16,1]{0,2,1:T(1,128)}), s32[32,16,1]{0,2,1:T(1,128)S(1)}, u32[]{:S(2)}, u32[]{:S(2)}) async-start(s32[32,16,1]{0,2,1:T(1,128)} %copy.56), calls=%async_computation.1 | async-start | bytes 16384 | tf_op jit(solution)/shard_map/all_to_all | solution.py:66
  9.0 2.8 %copy.54 = bf16[32,16,1024]{2,0,1:T(8,128)(2,1)} copy(bf16[32,16,1024]{2,1,0:T(8,128)(2,1)} %bitcast.44) | data formatting | bytes 2097152 | tf_op jit(solution)/shard_map/reshape | solution.py:60
  11.9 3.5 %all-to-all-done.1 = s32[32,16,1]{0,2,1:T(1,128)S(1)} async-done(((s32[32,16,1]{0,2,1:T(1,128)}), s32[32,16,1]{0,2,1:T(1,128)S(1)}, u32[]{:S(2)}, u32[]{:S(2)}) %all-to-all-start.1) | async-done | bytes 2080 | tf_op jit(solution)/shard_map/all_to_all | solution.py:66
  15.3 4.3 %all-to-all-start = ((bf16[32,16,1024]{2,0,1:T(8,128)(2,1)}), bf16[32,16,1024]{2,0,1:T(8,128)(2,1)}, u32[]{:S(2)}, u32[]{:S(2)}) async-start(bf16[32,16,1024]{2,0,1:T(8,128)(2,1)} %copy.54), calls=%async_computation | async-start | bytes 2097152 | tf_op jit(solution)/shard_map/all_to_all | solution.py:59
  19.9 2.0 %fusion.12 = bf16[16,1024]{1,0:T(8,128)(2,1)S(1)} fusion(bf16[16,1024]{1,0:T(8,128)(2,1)S(1)} %copy-done.1, bf16[1024,1024]{1,0:T(8,128)(2,1)} %param.16), kind=kOutput, calls=%fused_computation.28 | convolution fusion | flops 33587200 | bytes 2162688 | tf_op jit(solution)/shard_map/dot_general | solution.py:92
  22.1 2.4 %scatter_custom_fusion = s32[512]{0:T(512)S(1)} fusion(s32[512]{0:T(512)S(1)} %bitcast.45, s32[512]{0:T(512)S(1)} %iota.19, s32[]{:T(128)} %constant.23.clone.1), kind=kCustom, calls=%fused_computation.49 | custom fusion | bytes 2052 | tf_op jit(solution)/shard_map/scatter | solution.py:77
  24.6 18.0 %all-to-all-done = bf16[32,16,1024]{2,0,1:T(8,128)(2,1)} async-done(((bf16[32,16,1024]{2,0,1:T(8,128)(2,1)}), bf16[32,16,1024]{2,0,1:T(8,128)(2,1)}, u32[]{:S(2)}, u32[]{:S(2)}) %all-to-all-start) | async-done | bytes 1048608 | tf_op jit(solution)/shard_map/all_to_all | solution.py:59
  42.6 1.8 %copy.55 = bf16[32,16,1024]{2,1,0:T(8,128)(2,1)S(1)} copy(bf16[32,16,1024]{2,0,1:T(8,128)(2,1)} %all-to-all-done) | data formatting | bytes 2097152 | tf_op jit(solution)/shard_map/all_to_all | solution.py:59
  44.4 2.8 %gather_fusion = bf16[512,1024]{1,0:T(8,128)(2,1)} fusion(bf16[512,1024]{1,0:T(8,128)(2,1)S(1)} %bitcast.40, s32[1024]{0:T(1024)S(1)} %pad_clamp_fusion), kind=kCustom, calls=%fused_computation | custom fusion | bytes 2099200 | tf_op jit(solution)/shard_map/gather | solution.py:79
  47.2 1.5 fusion.9
  49.6 2.1 %convolution_convert_fusion = bf16[128,1024]{1,0:T(8,128)(2,1)S(1)} fusion(bf16[1024,1024]{1,0:T(8,128)(2,1)} %param.18, f32[128,1024]{1,0:T(8,128)S(1)} %fusion.9, f32[1024]{0:T(1024)} %copy-done.2, f32[128]{0:T(128)} %copy-done.4), kind=kOutput, calls=%fused_computation.20 | convolution fusion | flops 268959744 | bytes 2888192 | tf_op jit(solution)/shard_map/dot_general | solution.py:88
  51.9 118.4 %while.17 = (s32[]{:T(128)}, bf16[16,1024]{1,0:T(8,128)(2,1)S(1)}, f32[16,16]{0,1:T(8,128)S(1)}, f32[16,16]{0,1:T(8,128)S(1)}, f32[16,1024]{1,0:T(8,128)S(1)}, /...) while((s32[]{:T(128)}, bf16[16,1024]{1,0:T(8,128)(2,1)S(1)}, ...), condition=%wide.region_6.7_spmd.clone, body=%wide.region_3.6_spmd.clone.sunk | while | flops 8636675 | bytes 1955081 | solution.py:104
  53.7 1.3 collective-permute-start
  55.8 2.2 %collective-permute-start.2 = (bf16[16,16]{0,1:T(8,128)(2,1)S(1)}, bf16[16,16]{0,1:T(8,128)(2,1)S(1)}, u32[]{:S(2)}, u32[]{:S(2)}) collective-permute-start(bf16[16,16]{0,1:T(8,128)(2,1)S(1)} %get-tuple-element.157), channel_id=1, source_target_pairs={{15,0},{0,1},{1,2},{2,3},{3,4},{4,5},{5,6},{6,7},{7,8},{8,9},{9,10... | collective-permute-start | bytes 1544 | tf_op jit(solution)/shard_map/while/body/eval_jaxpr/ppermute | solution.py:13
  58.0 2.7 %collective-permute-done.1 = bf16[16,16]{0,1:T(8,128)(2,1)S(1)} collective-permute-done((bf16[16,16]{0,1:T(8,128)(2,1)S(1)}, bf16[16,16]{0,1:T(8,128)(2,1)S(1)}, u32[]{:S(2)}, u32[]{:S(2)}) %collective-permute-start.1) | collective-permute-done | bytes 544 | tf_op jit(solution)/shard_map/while/body/eval_jaxpr/ppermute | solution.py:13
  63.1 2.5 %collective-permute-start.2 = (bf16[16,16]{0,1:T(8,128)(2,1)S(1)}, bf16[16,16]{0,1:T(8,128)(2,1)S(1)}, u32[]{:S(2)}, u32[]{:S(2)}) collective-permute-start(bf16[16,16]{0,1:T(8,128)(2,1)S(1)} %get-tuple-element.157), channel_id=1, source_target_pairs={{15,0},{0,1},{1,2},{2,3},{3,4},{4,5},{5,6},{6,7},{7,8},{8,9},{9,10... | collective-permute-start | bytes 1544 | tf_op jit(solution)/shard_map/while/body/eval_jaxpr/ppermute | solution.py:13
  65.6 3.6 %collective-permute-done.1 = bf16[16,16]{0,1:T(8,128)(2,1)S(1)} collective-permute-done((bf16[16,16]{0,1:T(8,128)(2,1)S(1)}, bf16[16,16]{0,1:T(8,128)(2,1)S(1)}, u32[]{:S(2)}, u32[]{:S(2)}) %collective-permute-start.1) | collective-permute-done | bytes 544 | tf_op jit(solution)/shard_map/while/body/eval_jaxpr/ppermute | solution.py:13
  71.8 5.2 %collective-permute-done.1 = bf16[16,16]{0,1:T(8,128)(2,1)S(1)} collective-permute-done((bf16[16,16]{0,1:T(8,128)(2,1)S(1)}, bf16[16,16]{0,1:T(8,128)(2,1)S(1)}, u32[]{:S(2)}, u32[]{:S(2)}) %collective-permute-start.1) | collective-permute-done | bytes 544 | tf_op jit(solution)/shard_map/while/body/eval_jaxpr/ppermute | solution.py:13
  78.5 6.2 %collective-permute-done.1 = bf16[16,16]{0,1:T(8,128)(2,1)S(1)} collective-permute-done((bf16[16,16]{0,1:T(8,128)(2,1)S(1)}, bf16[16,16]{0,1:T(8,128)(2,1)S(1)}, u32[]{:S(2)}, u32[]{:S(2)}) %collective-permute-start.1) | collective-permute-done | bytes 544 | tf_op jit(solution)/shard_map/while/body/eval_jaxpr/ppermute | solution.py:13
  86.3 6.2 %collective-permute-done.1 = bf16[16,16]{0,1:T(8,128)(2,1)S(1)} collective-permute-done((bf16[16,16]{0,1:T(8,128)(2,1)S(1)}, bf16[16,16]{0,1:T(8,128)(2,1)S(1)}, u32[]{:S(2)}, u32[]{:S(2)}) %collective-permute-start.1) | collective-permute-done | bytes 544 | tf_op jit(solution)/shard_map/while/body/eval_jaxpr/ppermute | solution.py:13
  94.1 6.2 %collective-permute-done.1 = bf16[16,16]{0,1:T(8,128)(2,1)S(1)} collective-permute-done((bf16[16,16]{0,1:T(8,128)(2,1)S(1)}, bf16[16,16]{0,1:T(8,128)(2,1)S(1)}, u32[]{:S(2)}, u32[]{:S(2)}) %collective-permute-start.1) | collective-permute-done | bytes 544 | tf_op jit(solution)/shard_map/while/body/eval_jaxpr/ppermute | solution.py:13
  101.8 6.2 %collective-permute-done.1 = bf16[16,16]{0,1:T(8,128)(2,1)S(1)} collective-permute-done((bf16[16,16]{0,1:T(8,128)(2,1)S(1)}, bf16[16,16]{0,1:T(8,128)(2,1)S(1)}, u32[]{:S(2)}, u32[]{:S(2)}) %collective-permute-start.1) | collective-permute-done | bytes 544 | tf_op jit(solution)/shard_map/while/body/eval_jaxpr/ppermute | solution.py:13
  109.6 6.2 %collective-permute-done.1 = bf16[16,16]{0,1:T(8,128)(2,1)S(1)} collective-permute-done((bf16[16,16]{0,1:T(8,128)(2,1)S(1)}, bf16[16,16]{0,1:T(8,128)(2,1)S(1)}, u32[]{:S(2)}, u32[]{:S(2)}) %collective-permute-start.1) | collective-permute-done | bytes 544 | tf_op jit(solution)/shard_map/while/body/eval_jaxpr/ppermute | solution.py:13
  117.3 6.2 %collective-permute-done.1 = bf16[16,16]{0,1:T(8,128)(2,1)S(1)} collective-permute-done((bf16[16,16]{0,1:T(8,128)(2,1)S(1)}, bf16[16,16]{0,1:T(8,128)(2,1)S(1)}, u32[]{:S(2)}, u32[]{:S(2)}) %collective-permute-start.1) | collective-permute-done | bytes 544 | tf_op jit(solution)/shard_map/while/body/eval_jaxpr/ppermute | solution.py:13
  125.1 6.2 %collective-permute-done.1 = bf16[16,16]{0,1:T(8,128)(2,1)S(1)} collective-permute-done((bf16[16,16]{0,1:T(8,128)(2,1)S(1)}, bf16[16,16]{0,1:T(8,128)(2,1)S(1)}, u32[]{:S(2)}, u32[]{:S(2)}) %collective-permute-start.1) | collective-permute-done | bytes 544 | tf_op jit(solution)/shard_map/while/body/eval_jaxpr/ppermute | solution.py:13
  132.9 6.2 %collective-permute-done.1 = bf16[16,16]{0,1:T(8,128)(2,1)S(1)} collective-permute-done((bf16[16,16]{0,1:T(8,128)(2,1)S(1)}, bf16[16,16]{0,1:T(8,128)(2,1)S(1)}, u32[]{:S(2)}, u32[]{:S(2)}) %collective-permute-start.1) | collective-permute-done | bytes 544 | tf_op jit(solution)/shard_map/while/body/eval_jaxpr/ppermute | solution.py:13
  140.6 6.2 %collective-permute-done.1 = bf16[16,16]{0,1:T(8,128)(2,1)S(1)} collective-permute-done((bf16[16,16]{0,1:T(8,128)(2,1)S(1)}, bf16[16,16]{0,1:T(8,128)(2,1)S(1)}, u32[]{:S(2)}, u32[]{:S(2)}) %collective-permute-start.1) | collective-permute-done | bytes 544 | tf_op jit(solution)/shard_map/while/body/eval_jaxpr/ppermute | solution.py:13
  148.4 6.2 %collective-permute-done.1 = bf16[16,16]{0,1:T(8,128)(2,1)S(1)} collective-permute-done((bf16[16,16]{0,1:T(8,128)(2,1)S(1)}, bf16[16,16]{0,1:T(8,128)(2,1)S(1)}, u32[]{:S(2)}, u32[]{:S(2)}) %collective-permute-start.1) | collective-permute-done | bytes 544 | tf_op jit(solution)/shard_map/while/body/eval_jaxpr/ppermute | solution.py:13
  156.2 6.2 %collective-permute-done.1 = bf16[16,16]{0,1:T(8,128)(2,1)S(1)} collective-permute-done((bf16[16,16]{0,1:T(8,128)(2,1)S(1)}, bf16[16,16]{0,1:T(8,128)(2,1)S(1)}, u32[]{:S(2)}, u32[]{:S(2)}) %collective-permute-start.1) | collective-permute-done | bytes 544 | tf_op jit(solution)/shard_map/while/body/eval_jaxpr/ppermute | solution.py:13
  163.9 6.2 %collective-permute-done.1 = bf16[16,16]{0,1:T(8,128)(2,1)S(1)} collective-permute-done((bf16[16,16]{0,1:T(8,128)(2,1)S(1)}, bf16[16,16]{0,1:T(8,128)(2,1)S(1)}, u32[]{:S(2)}, u32[]{:S(2)}) %collective-permute-start.1) | collective-permute-done | bytes 544 | tf_op jit(solution)/shard_map/while/body/eval_jaxpr/ppermute | solution.py:13
  171.5 6.0 %collective-permute-done.5 = bf16[16,16]{0,1:T(8,128)(2,1)S(1)} collective-permute-done((bf16[16,16]{0,1:T(8,128)(2,1)S(1)}, bf16[16,16]{0,1:T(8,128)(2,1)S(1)}, u32[]{:S(2)}, u32[]{:S(2)}) %collective-permute-start.5) | collective-permute-done | bytes 544 | tf_op jit(solution)/shard_map/ppermute | solution.py:13
  177.8 2.6 %fusion.13 = bf16[16,1024]{1,0:T(8,128)(2,1)} fusion(bf16[1024,1024]{1,0:T(8,128)(2,1)} %param.19, bf16[16,1024]{1,0:T(8,128)(2,1)S(1)} %copy-done.1, f32[16,1024]{1,0:T(8,128)S(1)} %div.36, bf16[16,1024]{1,0:T(8,128)(2,1)S(1)} %collective-permute-done.4), kind=kOutput, calls=%fused_computation.29 | convolution fusion | flops 33652736 | bytes 2260992 | tf_op jit(solution)/shard_map/dot_general | solution.py:111
  (361 shorter events, 28.9 us)
Async XLA Ops:
  1.6 13.7 %all-to-all-start.1 = ((s32[32,16,1]{0,2,1:T(1,128)}), s32[32,16,1]{0,2,1:T(1,128)S(1)}, u32[]{:S(2)}, u32[]{:S(2)}) async-start(s32[32,16,1]{0,2,1:T(1,128)} %copy.56), calls=%async_computation.1 | async-start | bytes 16384 | tf_op jit(solution)/shard_map/all_to_all | solution.py:66
  15.3 27.3 %all-to-all-start = ((bf16[32,16,1024]{2,0,1:T(8,128)(2,1)}), bf16[32,16,1024]{2,0,1:T(8,128)(2,1)}, u32[]{:S(2)}, u32[]{:S(2)}) async-start(bf16[32,16,1024]{2,0,1:T(8,128)(2,1)} %copy.54), calls=%async_computation | async-start | bytes 2097152 | tf_op jit(solution)/shard_map/all_to_all | solution.py:59
  53.1 8.5 %collective-permute-start.3 = (bf16[16,1024]{1,0:T(8,128)(2,1)S(1)}, bf16[16,1024]{1,0:T(8,128)(2,1)S(1)}, u32[]{:S(2)}, u32[]{:S(2)}) collective-permute-start(bf16[16,1024]{1,0:T(8,128)(2,1)S(1)} %convert_element_type.136), channel_id=1, source_target_pairs={{15,0},{0,1},{1,2},{2,3},{3,4},{4,5},{5,6},{6,7},{7,8},{8,9},{9,10... | collective-permute-start | bytes 98312 | tf_op jit(solution)/shard_map/while/body/eval_jaxpr/ppermute | solution.py:13
  53.7 7.8 %collective-permute-start = (bf16[16,1024]{1,0:T(8,128)(2,1)S(1)}, bf16[16,1024]{1,0:T(8,128)(2,1)S(1)}, u32[]{:S(2)}, u32[]{:S(2)}) collective-permute-start(bf16[16,1024]{1,0:T(8,128)(2,1)S(1)} %copy.90), channel_id=1, source_target_pairs={{15,0},{0,1},{1,2},{2,3},{3,4},{4,5},{5,6},{6,7},{7,8},{8,9},{9,10... | collective-permute-start | bytes 98312 | tf_op jit(solution)/shard_map/while/body/eval_jaxpr/ppermute | solution.py:13
  62.7 6.5 %collective-permute-start.3 = (bf16[16,1024]{1,0:T(8,128)(2,1)S(1)}, bf16[16,1024]{1,0:T(8,128)(2,1)S(1)}, u32[]{:S(2)}, u32[]{:S(2)}) collective-permute-start(bf16[16,1024]{1,0:T(8,128)(2,1)S(1)} %convert_element_type.136), channel_id=1, source_target_pairs={{15,0},{0,1},{1,2},{2,3},{3,4},{4,5},{5,6},{6,7},{7,8},{8,9},{9,10... | collective-permute-start | bytes 98312 | tf_op jit(solution)/shard_map/while/body/eval_jaxpr/ppermute | solution.py:13
  62.8 6.5 %collective-permute-start = (bf16[16,1024]{1,0:T(8,128)(2,1)S(1)}, bf16[16,1024]{1,0:T(8,128)(2,1)S(1)}, u32[]{:S(2)}, u32[]{:S(2)}) collective-permute-start(bf16[16,1024]{1,0:T(8,128)(2,1)S(1)} %copy.90), channel_id=1, source_target_pairs={{15,0},{0,1},{1,2},{2,3},{3,4},{4,5},{5,6},{6,7},{7,8},{8,9},{9,10... | collective-permute-start | bytes 98312 | tf_op jit(solution)/shard_map/while/body/eval_jaxpr/ppermute | solution.py:13
  70.5 6.5 %collective-permute-start.3 = (bf16[16,1024]{1,0:T(8,128)(2,1)S(1)}, bf16[16,1024]{1,0:T(8,128)(2,1)S(1)}, u32[]{:S(2)}, u32[]{:S(2)}) collective-permute-start(bf16[16,1024]{1,0:T(8,128)(2,1)S(1)} %convert_element_type.136), channel_id=1, source_target_pairs={{15,0},{0,1},{1,2},{2,3},{3,4},{4,5},{5,6},{6,7},{7,8},{8,9},{9,10... | collective-permute-start | bytes 98312 | tf_op jit(solution)/shard_map/while/body/eval_jaxpr/ppermute | solution.py:13
  70.6 6.5 %collective-permute-start = (bf16[16,1024]{1,0:T(8,128)(2,1)S(1)}, bf16[16,1024]{1,0:T(8,128)(2,1)S(1)}, u32[]{:S(2)}, u32[]{:S(2)}) collective-permute-start(bf16[16,1024]{1,0:T(8,128)(2,1)S(1)} %copy.90), channel_id=1, source_target_pairs={{15,0},{0,1},{1,2},{2,3},{3,4},{4,5},{5,6},{6,7},{7,8},{8,9},{9,10... | collective-permute-start | bytes 98312 | tf_op jit(solution)/shard_map/while/body/eval_jaxpr/ppermute | solution.py:13
  78.3 6.5 %collective-permute-start.3 = (bf16[16,1024]{1,0:T(8,128)(2,1)S(1)}, bf16[16,1024]{1,0:T(8,128)(2,1)S(1)}, u32[]{:S(2)}, u32[]{:S(2)}) collective-permute-start(bf16[16,1024]{1,0:T(8,128)(2,1)S(1)} %convert_element_type.136), channel_id=1, source_target_pairs={{15,0},{0,1},{1,2},{2,3},{3,4},{4,5},{5,6},{6,7},{7,8},{8,9},{9,10... | collective-permute-start | bytes 98312 | tf_op jit(solution)/shard_map/while/body/eval_jaxpr/ppermute | solution.py:13
  78.3 6.5 %collective-permute-start = (bf16[16,1024]{1,0:T(8,128)(2,1)S(1)}, bf16[16,1024]{1,0:T(8,128)(2,1)S(1)}, u32[]{:S(2)}, u32[]{:S(2)}) collective-permute-start(bf16[16,1024]{1,0:T(8,128)(2,1)S(1)} %copy.90), channel_id=1, source_target_pairs={{15,0},{0,1},{1,2},{2,3},{3,4},{4,5},{5,6},{6,7},{7,8},{8,9},{9,10... | collective-permute-start | bytes 98312 | tf_op jit(solution)/shard_map/while/body/eval_jaxpr/ppermute | solution.py:13
  86.0 6.5 %collective-permute-start.3 = (bf16[16,1024]{1,0:T(8,128)(2,1)S(1)}, bf16[16,1024]{1,0:T(8,128)(2,1)S(1)}, u32[]{:S(2)}, u32[]{:S(2)}) collective-permute-start(bf16[16,1024]{1,0:T(8,128)(2,1)S(1)} %convert_element_type.136), channel_id=1, source_target_pairs={{15,0},{0,1},{1,2},{2,3},{3,4},{4,5},{5,6},{6,7},{7,8},{8,9},{9,10... | collective-permute-start | bytes 98312 | tf_op jit(solution)/shard_map/while/body/eval_jaxpr/ppermute | solution.py:13
  86.1 6.5 %collective-permute-start = (bf16[16,1024]{1,0:T(8,128)(2,1)S(1)}, bf16[16,1024]{1,0:T(8,128)(2,1)S(1)}, u32[]{:S(2)}, u32[]{:S(2)}) collective-permute-start(bf16[16,1024]{1,0:T(8,128)(2,1)S(1)} %copy.90), channel_id=1, source_target_pairs={{15,0},{0,1},{1,2},{2,3},{3,4},{4,5},{5,6},{6,7},{7,8},{8,9},{9,10... | collective-permute-start | bytes 98312 | tf_op jit(solution)/shard_map/while/body/eval_jaxpr/ppermute | solution.py:13
  93.8 6.5 %collective-permute-start.3 = (bf16[16,1024]{1,0:T(8,128)(2,1)S(1)}, bf16[16,1024]{1,0:T(8,128)(2,1)S(1)}, u32[]{:S(2)}, u32[]{:S(2)}) collective-permute-start(bf16[16,1024]{1,0:T(8,128)(2,1)S(1)} %convert_element_type.136), channel_id=1, source_target_pairs={{15,0},{0,1},{1,2},{2,3},{3,4},{4,5},{5,6},{6,7},{7,8},{8,9},{9,10... | collective-permute-start | bytes 98312 | tf_op jit(solution)/shard_map/while/body/eval_jaxpr/ppermute | solution.py:13
  93.9 6.5 %collective-permute-start = (bf16[16,1024]{1,0:T(8,128)(2,1)S(1)}, bf16[16,1024]{1,0:T(8,128)(2,1)S(1)}, u32[]{:S(2)}, u32[]{:S(2)}) collective-permute-start(bf16[16,1024]{1,0:T(8,128)(2,1)S(1)} %copy.90), channel_id=1, source_target_pairs={{15,0},{0,1},{1,2},{2,3},{3,4},{4,5},{5,6},{6,7},{7,8},{8,9},{9,10... | collective-permute-start | bytes 98312 | tf_op jit(solution)/shard_map/while/body/eval_jaxpr/ppermute | solution.py:13
  101.6 6.5 %collective-permute-start.3 = (bf16[16,1024]{1,0:T(8,128)(2,1)S(1)}, bf16[16,1024]{1,0:T(8,128)(2,1)S(1)}, u32[]{:S(2)}, u32[]{:S(2)}) collective-permute-start(bf16[16,1024]{1,0:T(8,128)(2,1)S(1)} %convert_element_type.136), channel_id=1, source_target_pairs={{15,0},{0,1},{1,2},{2,3},{3,4},{4,5},{5,6},{6,7},{7,8},{8,9},{9,10... | collective-permute-start | bytes 98312 | tf_op jit(solution)/shard_map/while/body/eval_jaxpr/ppermute | solution.py:13
  101.6 6.5 %collective-permute-start = (bf16[16,1024]{1,0:T(8,128)(2,1)S(1)}, bf16[16,1024]{1,0:T(8,128)(2,1)S(1)}, u32[]{:S(2)}, u32[]{:S(2)}) collective-permute-start(bf16[16,1024]{1,0:T(8,128)(2,1)S(1)} %copy.90), channel_id=1, source_target_pairs={{15,0},{0,1},{1,2},{2,3},{3,4},{4,5},{5,6},{6,7},{7,8},{8,9},{9,10... | collective-permute-start | bytes 98312 | tf_op jit(solution)/shard_map/while/body/eval_jaxpr/ppermute | solution.py:13
  109.3 6.5 %collective-permute-start.3 = (bf16[16,1024]{1,0:T(8,128)(2,1)S(1)}, bf16[16,1024]{1,0:T(8,128)(2,1)S(1)}, u32[]{:S(2)}, u32[]{:S(2)}) collective-permute-start(bf16[16,1024]{1,0:T(8,128)(2,1)S(1)} %convert_element_type.136), channel_id=1, source_target_pairs={{15,0},{0,1},{1,2},{2,3},{3,4},{4,5},{5,6},{6,7},{7,8},{8,9},{9,10... | collective-permute-start | bytes 98312 | tf_op jit(solution)/shard_map/while/body/eval_jaxpr/ppermute | solution.py:13
  109.4 6.5 %collective-permute-start = (bf16[16,1024]{1,0:T(8,128)(2,1)S(1)}, bf16[16,1024]{1,0:T(8,128)(2,1)S(1)}, u32[]{:S(2)}, u32[]{:S(2)}) collective-permute-start(bf16[16,1024]{1,0:T(8,128)(2,1)S(1)} %copy.90), channel_id=1, source_target_pairs={{15,0},{0,1},{1,2},{2,3},{3,4},{4,5},{5,6},{6,7},{7,8},{8,9},{9,10... | collective-permute-start | bytes 98312 | tf_op jit(solution)/shard_map/while/body/eval_jaxpr/ppermute | solution.py:13
  117.1 6.5 %collective-permute-start.3 = (bf16[16,1024]{1,0:T(8,128)(2,1)S(1)}, bf16[16,1024]{1,0:T(8,128)(2,1)S(1)}, u32[]{:S(2)}, u32[]{:S(2)}) collective-permute-start(bf16[16,1024]{1,0:T(8,128)(2,1)S(1)} %convert_element_type.136), channel_id=1, source_target_pairs={{15,0},{0,1},{1,2},{2,3},{3,4},{4,5},{5,6},{6,7},{7,8},{8,9},{9,10... | collective-permute-start | bytes 98312 | tf_op jit(solution)/shard_map/while/body/eval_jaxpr/ppermute | solution.py:13
  117.1 6.5 %collective-permute-start = (bf16[16,1024]{1,0:T(8,128)(2,1)S(1)}, bf16[16,1024]{1,0:T(8,128)(2,1)S(1)}, u32[]{:S(2)}, u32[]{:S(2)}) collective-permute-start(bf16[16,1024]{1,0:T(8,128)(2,1)S(1)} %copy.90), channel_id=1, source_target_pairs={{15,0},{0,1},{1,2},{2,3},{3,4},{4,5},{5,6},{6,7},{7,8},{8,9},{9,10... | collective-permute-start | bytes 98312 | tf_op jit(solution)/shard_map/while/body/eval_jaxpr/ppermute | solution.py:13
  124.8 6.5 %collective-permute-start.3 = (bf16[16,1024]{1,0:T(8,128)(2,1)S(1)}, bf16[16,1024]{1,0:T(8,128)(2,1)S(1)}, u32[]{:S(2)}, u32[]{:S(2)}) collective-permute-start(bf16[16,1024]{1,0:T(8,128)(2,1)S(1)} %convert_element_type.136), channel_id=1, source_target_pairs={{15,0},{0,1},{1,2},{2,3},{3,4},{4,5},{5,6},{6,7},{7,8},{8,9},{9,10... | collective-permute-start | bytes 98312 | tf_op jit(solution)/shard_map/while/body/eval_jaxpr/ppermute | solution.py:13
  124.9 6.5 %collective-permute-start = (bf16[16,1024]{1,0:T(8,128)(2,1)S(1)}, bf16[16,1024]{1,0:T(8,128)(2,1)S(1)}, u32[]{:S(2)}, u32[]{:S(2)}) collective-permute-start(bf16[16,1024]{1,0:T(8,128)(2,1)S(1)} %copy.90), channel_id=1, source_target_pairs={{15,0},{0,1},{1,2},{2,3},{3,4},{4,5},{5,6},{6,7},{7,8},{8,9},{9,10... | collective-permute-start | bytes 98312 | tf_op jit(solution)/shard_map/while/body/eval_jaxpr/ppermute | solution.py:13
  132.6 6.5 %collective-permute-start.3 = (bf16[16,1024]{1,0:T(8,128)(2,1)S(1)}, bf16[16,1024]{1,0:T(8,128)(2,1)S(1)}, u32[]{:S(2)}, u32[]{:S(2)}) collective-permute-start(bf16[16,1024]{1,0:T(8,128)(2,1)S(1)} %convert_element_type.136), channel_id=1, source_target_pairs={{15,0},{0,1},{1,2},{2,3},{3,4},{4,5},{5,6},{6,7},{7,8},{8,9},{9,10... | collective-permute-start | bytes 98312 | tf_op jit(solution)/shard_map/while/body/eval_jaxpr/ppermute | solution.py:13
  132.7 6.5 %collective-permute-start = (bf16[16,1024]{1,0:T(8,128)(2,1)S(1)}, bf16[16,1024]{1,0:T(8,128)(2,1)S(1)}, u32[]{:S(2)}, u32[]{:S(2)}) collective-permute-start(bf16[16,1024]{1,0:T(8,128)(2,1)S(1)} %copy.90), channel_id=1, source_target_pairs={{15,0},{0,1},{1,2},{2,3},{3,4},{4,5},{5,6},{6,7},{7,8},{8,9},{9,10... | collective-permute-start | bytes 98312 | tf_op jit(solution)/shard_map/while/body/eval_jaxpr/ppermute | solution.py:13
  140.4 6.5 %collective-permute-start.3 = (bf16[16,1024]{1,0:T(8,128)(2,1)S(1)}, bf16[16,1024]{1,0:T(8,128)(2,1)S(1)}, u32[]{:S(2)}, u32[]{:S(2)}) collective-permute-start(bf16[16,1024]{1,0:T(8,128)(2,1)S(1)} %convert_element_type.136), channel_id=1, source_target_pairs={{15,0},{0,1},{1,2},{2,3},{3,4},{4,5},{5,6},{6,7},{7,8},{8,9},{9,10... | collective-permute-start | bytes 98312 | tf_op jit(solution)/shard_map/while/body/eval_jaxpr/ppermute | solution.py:13
  140.4 6.5 %collective-permute-start = (bf16[16,1024]{1,0:T(8,128)(2,1)S(1)}, bf16[16,1024]{1,0:T(8,128)(2,1)S(1)}, u32[]{:S(2)}, u32[]{:S(2)}) collective-permute-start(bf16[16,1024]{1,0:T(8,128)(2,1)S(1)} %copy.90), channel_id=1, source_target_pairs={{15,0},{0,1},{1,2},{2,3},{3,4},{4,5},{5,6},{6,7},{7,8},{8,9},{9,10... | collective-permute-start | bytes 98312 | tf_op jit(solution)/shard_map/while/body/eval_jaxpr/ppermute | solution.py:13
  148.1 6.5 %collective-permute-start.3 = (bf16[16,1024]{1,0:T(8,128)(2,1)S(1)}, bf16[16,1024]{1,0:T(8,128)(2,1)S(1)}, u32[]{:S(2)}, u32[]{:S(2)}) collective-permute-start(bf16[16,1024]{1,0:T(8,128)(2,1)S(1)} %convert_element_type.136), channel_id=1, source_target_pairs={{15,0},{0,1},{1,2},{2,3},{3,4},{4,5},{5,6},{6,7},{7,8},{8,9},{9,10... | collective-permute-start | bytes 98312 | tf_op jit(solution)/shard_map/while/body/eval_jaxpr/ppermute | solution.py:13
  148.2 6.5 %collective-permute-start = (bf16[16,1024]{1,0:T(8,128)(2,1)S(1)}, bf16[16,1024]{1,0:T(8,128)(2,1)S(1)}, u32[]{:S(2)}, u32[]{:S(2)}) collective-permute-start(bf16[16,1024]{1,0:T(8,128)(2,1)S(1)} %copy.90), channel_id=1, source_target_pairs={{15,0},{0,1},{1,2},{2,3},{3,4},{4,5},{5,6},{6,7},{7,8},{8,9},{9,10... | collective-permute-start | bytes 98312 | tf_op jit(solution)/shard_map/while/body/eval_jaxpr/ppermute | solution.py:13
  155.9 6.5 %collective-permute-start.3 = (bf16[16,1024]{1,0:T(8,128)(2,1)S(1)}, bf16[16,1024]{1,0:T(8,128)(2,1)S(1)}, u32[]{:S(2)}, u32[]{:S(2)}) collective-permute-start(bf16[16,1024]{1,0:T(8,128)(2,1)S(1)} %convert_element_type.136), channel_id=1, source_target_pairs={{15,0},{0,1},{1,2},{2,3},{3,4},{4,5},{5,6},{6,7},{7,8},{8,9},{9,10... | collective-permute-start | bytes 98312 | tf_op jit(solution)/shard_map/while/body/eval_jaxpr/ppermute | solution.py:13
  156.0 6.5 %collective-permute-start = (bf16[16,1024]{1,0:T(8,128)(2,1)S(1)}, bf16[16,1024]{1,0:T(8,128)(2,1)S(1)}, u32[]{:S(2)}, u32[]{:S(2)}) collective-permute-start(bf16[16,1024]{1,0:T(8,128)(2,1)S(1)} %copy.90), channel_id=1, source_target_pairs={{15,0},{0,1},{1,2},{2,3},{3,4},{4,5},{5,6},{6,7},{7,8},{8,9},{9,10... | collective-permute-start | bytes 98312 | tf_op jit(solution)/shard_map/while/body/eval_jaxpr/ppermute | solution.py:13
  163.7 6.5 %collective-permute-start.3 = (bf16[16,1024]{1,0:T(8,128)(2,1)S(1)}, bf16[16,1024]{1,0:T(8,128)(2,1)S(1)}, u32[]{:S(2)}, u32[]{:S(2)}) collective-permute-start(bf16[16,1024]{1,0:T(8,128)(2,1)S(1)} %convert_element_type.136), channel_id=1, source_target_pairs={{15,0},{0,1},{1,2},{2,3},{3,4},{4,5},{5,6},{6,7},{7,8},{8,9},{9,10... | collective-permute-start | bytes 98312 | tf_op jit(solution)/shard_map/while/body/eval_jaxpr/ppermute | solution.py:13
  163.7 6.5 %collective-permute-start = (bf16[16,1024]{1,0:T(8,128)(2,1)S(1)}, bf16[16,1024]{1,0:T(8,128)(2,1)S(1)}, u32[]{:S(2)}, u32[]{:S(2)}) collective-permute-start(bf16[16,1024]{1,0:T(8,128)(2,1)S(1)} %copy.90), channel_id=1, source_target_pairs={{15,0},{0,1},{1,2},{2,3},{3,4},{4,5},{5,6},{6,7},{7,8},{8,9},{9,10... | collective-permute-start | bytes 98312 | tf_op jit(solution)/shard_map/while/body/eval_jaxpr/ppermute | solution.py:13
  (38 other events, 312.1 us)
where the time goes:
time: 181 us; the launch traced here: 180 us
  waiting for transfers between devices  115 us (64%)
  starting transfers between devices  23.6 us (13%)
  local copies, waits for them, and re-layouts  17.7 us (10%)
  matrix products  16.3 us (9%)
  other arithmetic  5.59 us (3%)
    ppermute x62, waiting for transfers between devices, shifted(): return lax.ppermute(block, axis, route)  93.7 us
    all_to_all x1, waiting for transfers between devices, local(): lax.all_to_all(tokens.reshape(per_peer, cycle_size, model_width), 'blk',...  18 us
    ppermute x62, starting transfers between devices, shifted(): return lax.ppermute(block, axis, route)  11.9 us
    all_to_all x1, starting transfers between devices, local(): lax.all_to_all(patch_of_row.reshape(per_peer, cycle_size), 'blk', split_a...  7.39 us
    dot_general x16, matrix products, absorb(): jnp.einsum('lhk,khd->lhd', weights.astype(jnp.bfloat16), value_heads, pre...  5.02 us
    all_to_all x1, starting transfers between devices, local(): lax.all_to_all(tokens.reshape(per_peer, cycle_size, model_width), 'blk',...  4.33 us
    dot_general x16, matrix products, absorb(): jnp.einsum('lhd,khd->lhk', tile_heads, key_heads, preferred_element_type=...  4.1 us
  transfers between devices with their start and end apart: 64, of which 19 were waited for; matrix products, arithmetic and copies ran while one was open for 4% of the time, Pallas kernels for 0%

commit v1 on v0

--- a/solution.py
+++ b/solution.py
@@ -56,12 +56,18 @@
     head_width = model_width // head_count
     per_peer = tok_rows // cycle_size
     patches_dev = tok_rows // CONTRASTS
-    received = lax.all_to_all(
-        tokens.reshape(per_peer, cycle_size, model_width),
-        "blk",
-        split_axis=1,
-        concat_axis=1,
-        tiled=True,
+    received = jnp.concatenate(
+        lax.all_to_all(
+            jnp.stack(
+                jnp.split(
+                    tokens.reshape(per_peer, cycle_size, model_width), lax.axis_size("blk"), axis=1
+                )
+            ),
+            "blk",
+            0,
+            0,
+        ),
+        axis=1,
     )
     received_ids = lax.all_to_all(
         patch_of_row.reshape(per_peer, cycle_size), "blk", split_axis=1, concat_axis=1, tiled=True

time: 181 us -> 193 us (1.066)
  local copies, waits for them, and re-layouts: 17.7 us -> 31.2 us
  waiting for transfers between devices: 115 us -> 111 us
    unnamed x12 -> x25, local copies, waits for them, and re-layouts: 0.1 us -> 9.77 us
    split x0 -> x1, local copies, waits for them, and re-layouts: none -> 6.01 us  [local(): jnp.split(tokens.reshape(per_peer, cycle_size, model_width), lax.axis_siz...]
    all_to_all x1, waiting for transfers between devices: 3.46 us -> 0.01 us  [local(): lax.all_to_all(patch_of_row.reshape(per_peer, cycle_size), 'blk', split_a...]
  transfers between devices with their start and end apart: 64 -> 64, of which waited for: 19 -> 18; matrix products, arithmetic and copies ran while one was open for 4% -> 12% of each run, Pallas kernels for 0% -> 0%
where the time goes in v1:
time: 193 us; the launch traced here: 192 us
  waiting for transfers between devices  111 us (58%)
  local copies, waits for them, and re-layouts  31.2 us (16%)
  starting transfers between devices  25.3 us (13%)
  matrix products  16.3 us (8%)
  other arithmetic  6.18 us (3%)
    ppermute x62, waiting for transfers between devices, shifted(): return lax.ppermute(block, axis, route)  93.6 us
    all_to_all x1, waiting for transfers between devices, local(): lax.all_to_all(jnp.stack(jnp.split(tokens.reshape(per_peer, cycle_size, m...  17.5 us
    ppermute x62, starting transfers between devices, shifted(): return lax.ppermute(block, axis, route)  11.9 us
    unnamed x25, local copies, waits for them, and re-layouts  9.77 us
    all_to_all x1, starting transfers between devices, local(): lax.all_to_all(patch_of_row.reshape(per_peer, cycle_size), 'blk', split_a...  7.39 us
    all_to_all x1, starting transfers between devices, local(): lax.all_to_all(jnp.stack(jnp.split(tokens.reshape(per_peer, cycle_size, m...  6.04 us
    split x1, local copies, waits for them, and re-layouts, local(): jnp.split(tokens.reshape(per_peer, cycle_size, model_width), lax.axis_siz...  6.01 us
    dot_general x16, matrix products, absorb(): jnp.einsum('lhk,khd->lhd', weights.astype(jnp.bfloat16), value_heads, pre...  5.02 us
  transfers between devices with their start and end apart: 64, of which 18 were waited for; matrix products, arithmetic and copies ran while one was open for 12% of the time, Pallas kernels for 0%

profile of v1, /device:TPU:0, one launch (start us, length us, event | category | flops | bytes accessed | tf_op | source)
XLA Modules:
  0.0 192.2 jit_solution(8797374758111460095)
XLA Ops:
  1.6 7.4 %all-to-all-start.1 = ((s32[32,16,1]{0,2,1:T(1,128)}), s32[32,16,1]{0,2,1:T(1,128)S(1)}, u32[]{:S(2)}, u32[]{:S(2)}) async-start(s32[32,16,1]{0,2,1:T(1,128)} %copy.69), calls=%async_computation.1 | async-start | bytes 16384 | tf_op jit(solution)/shard_map/all_to_all | solution.py:72
  9.0 6.0 %fusion.23 = (bf16[32,1,1024]{2,1,0:T(2,128)(2,1)S(1)}, bf16[32,1,1024]{2,1,0:T(2,128)(2,1)S(1)}, bf16[32,1,1024]{2,1,0:T(2,128)(2,1)S(1)}, bf16[32,1,1024]{2,1,...) fusion(bf16[32,16,1024]{2,1,0:T(8,128)(2,1)} %bitcast.77), kind=kLoop, calls=%fused_computation.72 | loop fusion | bytes 2097152 | tf_op jit(solution)/shard_map/split | solution.py:62
  25.4 6.0 %all-to-all-start = ((bf16[16,32,1,1024]{3,1,2,0:T(8,128)(2,1)}), bf16[16,32,1,1024]{3,1,2,0:T(8,128)(2,1)}, u32[]{:S(2)}, u32[]{:S(2)}) async-start(bf16[16,32,1,1024]{3,1,2,0:T(8,128)(2,1)} %bitcast_dynamic-update-slice_fusion), calls=%async_computation | async-start | bytes 2097152 | tf_op jit(solution)/shard_map/all_to_all | solution.py:60
  32.3 2.0 %fusion.12 = bf16[16,1024]{1,0:T(8,128)(2,1)S(1)} fusion(bf16[16,1024]{1,0:T(8,128)(2,1)S(1)} %copy-done.1, bf16[1024,1024]{1,0:T(8,128)(2,1)} %param.16), kind=kOutput, calls=%fused_computation.28 | convolution fusion | flops 33587200 | bytes 2162688 | tf_op jit(solution)/shard_map/dot_general | solution.py:98
  34.5 2.4 %scatter_custom_fusion = s32[512]{0:T(512)S(1)} fusion(s32[512]{0:T(512)S(1)} %bitcast.78, s32[512]{0:T(512)S(1)} %iota.19, s32[]{:T(128)} %constant.23.clone.1), kind=kCustom, calls=%fused_computation.65 | custom fusion | bytes 2052 | tf_op jit(solution)/shard_map/scatter | solution.py:83
  37.0 17.5 %all-to-all-done = bf16[16,32,1,1024]{3,1,2,0:T(8,128)(2,1)} async-done(((bf16[16,32,1,1024]{3,1,2,0:T(8,128)(2,1)}), bf16[16,32,1,1024]{3,1,2,0:T(8,128)(2,1)}, u32[]{:S(2)}, u32[]{:S(2)}) %all-to-all-start) | async-done | bytes 1048608 | tf_op jit(solution)/shard_map/all_to_all | solution.py:60
  54.5 1.8 copy.68
  56.3 2.8 %gather_fusion = bf16[512,1024]{1,0:T(8,128)(2,1)} fusion(bf16[512,1024]{1,0:T(8,128)(2,1)S(1)} %bitcast.73, s32[1024]{0:T(1024)S(1)} %pad_clamp_fusion), kind=kCustom, calls=%fused_computation | custom fusion | bytes 2099200 | tf_op jit(solution)/shard_map/gather | solution.py:85
  59.0 1.5 fusion.9
  61.4 2.1 %convolution_convert_fusion.1 = bf16[128,1024]{1,0:T(8,128)(2,1)S(1)} fusion(bf16[1024,1024]{1,0:T(8,128)(2,1)} %param.17, f32[128,1024]{1,0:T(8,128)S(1)} %fusion.9, f32[1024]{0:T(1024)S(1)} %copy-done.2, f32[128]{0:T(128)S(1)} %add_rsqrt_fusion), kind=kOutput, calls=%fused_computation.21 | convolution fusion | flops 268959744 | bytes 2888192 | tf_op jit(solution)/shard_map/dot_general | solution.py:93
  63.6 118.4 %while.17 = (s32[]{:T(128)}, bf16[16,1024]{1,0:T(8,128)(2,1)S(1)}, f32[16,16]{0,1:T(8,128)S(1)}, f32[16,16]{0,1:T(8,128)S(1)}, f32[16,1024]{1,0:T(8,128)S(1)}, /...) while((s32[]{:T(128)}, bf16[16,1024]{1,0:T(8,128)(2,1)S(1)}, ...), condition=%wide.region_6.7_spmd.clone, body=%wide.region_3.6_spmd.clone.sunk | while | flops 8636675 | bytes 1955081 | solution.py:110
  65.5 1.3 collective-permute-start
  67.6 2.2 %collective-permute-start.1 = (bf16[16,16]{0,1:T(8,128)(2,1)S(1)}, bf16[16,16]{0,1:T(8,128)(2,1)S(1)}, u32[]{:S(2)}, u32[]{:S(2)}) collective-permute-start(bf16[16,16]{0,1:T(8,128)(2,1)S(1)} %get-tuple-element.170), channel_id=1, source_target_pairs={{15,0},{0,1},{1,2},{2,3},{3,4},{4,5},{5,6},{6,7},{7,8},{8,9},{9,10... | collective-permute-start | bytes 1544 | tf_op jit(solution)/shard_map/while/body/eval_jaxpr/ppermute | solution.py:13
  69.8 2.7 %collective-permute-done.2 = bf16[16,16]{0,1:T(8,128)(2,1)S(1)} collective-permute-done((bf16[16,16]{0,1:T(8,128)(2,1)S(1)}, bf16[16,16]{0,1:T(8,128)(2,1)S(1)}, u32[]{:S(2)}, u32[]{:S(2)}) %collective-permute-start.2) | collective-permute-done | bytes 544 | tf_op jit(solution)/shard_map/while/body/eval_jaxpr/ppermute | solution.py:13
  75.0 2.4 %collective-permute-start.1 = (bf16[16,16]{0,1:T(8,128)(2,1)S(1)}, bf16[16,16]{0,1:T(8,128)(2,1)S(1)}, u32[]{:S(2)}, u32[]{:S(2)}) collective-permute-start(bf16[16,16]{0,1:T(8,128)(2,1)S(1)} %get-tuple-element.170), channel_id=1, source_target_pairs={{15,0},{0,1},{1,2},{2,3},{3,4},{4,5},{5,6},{6,7},{7,8},{8,9},{9,10... | collective-permute-start | bytes 1544 | tf_op jit(solution)/shard_map/while/body/eval_jaxpr/ppermute | solution.py:13
  77.4 3.6 %collective-permute-done.2 = bf16[16,16]{0,1:T(8,128)(2,1)S(1)} collective-permute-done((bf16[16,16]{0,1:T(8,128)(2,1)S(1)}, bf16[16,16]{0,1:T(8,128)(2,1)S(1)}, u32[]{:S(2)}, u32[]{:S(2)}) %collective-permute-start.2) | collective-permute-done | bytes 544 | tf_op jit(solution)/shard_map/while/body/eval_jaxpr/ppermute | solution.py:13
  82.5 1.1 collective-permute-start.1
  83.6 5.2 %collective-permute-done.2 = bf16[16,16]{0,1:T(8,128)(2,1)S(1)} collective-permute-done((bf16[16,16]{0,1:T(8,128)(2,1)S(1)}, bf16[16,16]{0,1:T(8,128)(2,1)S(1)}, u32[]{:S(2)}, u32[]{:S(2)}) %collective-permute-start.2) | collective-permute-done | bytes 544 | tf_op jit(solution)/shard_map/while/body/eval_jaxpr/ppermute | solution.py:13
  90.3 6.2 %collective-permute-done.2 = bf16[16,16]{0,1:T(8,128)(2,1)S(1)} collective-permute-done((bf16[16,16]{0,1:T(8,128)(2,1)S(1)}, bf16[16,16]{0,1:T(8,128)(2,1)S(1)}, u32[]{:S(2)}, u32[]{:S(2)}) %collective-permute-start.2) | collective-permute-done | bytes 544 | tf_op jit(solution)/shard_map/while/body/eval_jaxpr/ppermute | solution.py:13
  98.1 6.2 %collective-permute-done.2 = bf16[16,16]{0,1:T(8,128)(2,1)S(1)} collective-permute-done((bf16[16,16]{0,1:T(8,128)(2,1)S(1)}, bf16[16,16]{0,1:T(8,128)(2,1)S(1)}, u32[]{:S(2)}, u32[]{:S(2)}) %collective-permute-start.2) | collective-permute-done | bytes 544 | tf_op jit(solution)/shard_map/while/body/eval_jaxpr/ppermute | solution.py:13
  105.9 6.2 %collective-permute-done.2 = bf16[16,16]{0,1:T(8,128)(2,1)S(1)} collective-permute-done((bf16[16,16]{0,1:T(8,128)(2,1)S(1)}, bf16[16,16]{0,1:T(8,128)(2,1)S(1)}, u32[]{:S(2)}, u32[]{:S(2)}) %collective-permute-start.2) | collective-permute-done | bytes 544 | tf_op jit(solution)/shard_map/while/body/eval_jaxpr/ppermute | solution.py:13
  113.6 6.2 %collective-permute-done.2 = bf16[16,16]{0,1:T(8,128)(2,1)S(1)} collective-permute-done((bf16[16,16]{0,1:T(8,128)(2,1)S(1)}, bf16[16,16]{0,1:T(8,128)(2,1)S(1)}, u32[]{:S(2)}, u32[]{:S(2)}) %collective-permute-start.2) | collective-permute-done | bytes 544 | tf_op jit(solution)/shard_map/while/body/eval_jaxpr/ppermute | solution.py:13
  121.4 6.2 %collective-permute-done.2 = bf16[16,16]{0,1:T(8,128)(2,1)S(1)} collective-permute-done((bf16[16,16]{0,1:T(8,128)(2,1)S(1)}, bf16[16,16]{0,1:T(8,128)(2,1)S(1)}, u32[]{:S(2)}, u32[]{:S(2)}) %collective-permute-start.2) | collective-permute-done | bytes 544 | tf_op jit(solution)/shard_map/while/body/eval_jaxpr/ppermute | solution.py:13
  129.1 6.2 %collective-permute-done.2 = bf16[16,16]{0,1:T(8,128)(2,1)S(1)} collective-permute-done((bf16[16,16]{0,1:T(8,128)(2,1)S(1)}, bf16[16,16]{0,1:T(8,128)(2,1)S(1)}, u32[]{:S(2)}, u32[]{:S(2)}) %collective-permute-start.2) | collective-permute-done | bytes 544 | tf_op jit(solution)/shard_map/while/body/eval_jaxpr/ppermute | solution.py:13
  136.9 6.2 %collective-permute-done.2 = bf16[16,16]{0,1:T(8,128)(2,1)S(1)} collective-permute-done((bf16[16,16]{0,1:T(8,128)(2,1)S(1)}, bf16[16,16]{0,1:T(8,128)(2,1)S(1)}, u32[]{:S(2)}, u32[]{:S(2)}) %collective-permute-start.2) | collective-permute-done | bytes 544 | tf_op jit(solution)/shard_map/while/body/eval_jaxpr/ppermute | solution.py:13
  144.7 6.2 %collective-permute-done.2 = bf16[16,16]{0,1:T(8,128)(2,1)S(1)} collective-permute-done((bf16[16,16]{0,1:T(8,128)(2,1)S(1)}, bf16[16,16]{0,1:T(8,128)(2,1)S(1)}, u32[]{:S(2)}, u32[]{:S(2)}) %collective-permute-start.2) | collective-permute-done | bytes 544 | tf_op jit(solution)/shard_map/while/body/eval_jaxpr/ppermute | solution.py:13
  152.4 6.2 %collective-permute-done.2 = bf16[16,16]{0,1:T(8,128)(2,1)S(1)} collective-permute-done((bf16[16,16]{0,1:T(8,128)(2,1)S(1)}, bf16[16,16]{0,1:T(8,128)(2,1)S(1)}, u32[]{:S(2)}, u32[]{:S(2)}) %collective-permute-start.2) | collective-permute-done | bytes 544 | tf_op jit(solution)/shard_map/while/body/eval_jaxpr/ppermute | solution.py:13
  160.2 6.2 %collective-permute-done.2 = bf16[16,16]{0,1:T(8,128)(2,1)S(1)} collective-permute-done((bf16[16,16]{0,1:T(8,128)(2,1)S(1)}, bf16[16,16]{0,1:T(8,128)(2,1)S(1)}, u32[]{:S(2)}, u32[]{:S(2)}) %collective-permute-start.2) | collective-permute-done | bytes 544 | tf_op jit(solution)/shard_map/while/body/eval_jaxpr/ppermute | solution.py:13
  168.0 6.2 %collective-permute-done.2 = bf16[16,16]{0,1:T(8,128)(2,1)S(1)} collective-permute-done((bf16[16,16]{0,1:T(8,128)(2,1)S(1)}, bf16[16,16]{0,1:T(8,128)(2,1)S(1)}, u32[]{:S(2)}, u32[]{:S(2)}) %collective-permute-start.2) | collective-permute-done | bytes 544 | tf_op jit(solution)/shard_map/while/body/eval_jaxpr/ppermute | solution.py:13
  175.7 6.2 %collective-permute-done.2 = bf16[16,16]{0,1:T(8,128)(2,1)S(1)} collective-permute-done((bf16[16,16]{0,1:T(8,128)(2,1)S(1)}, bf16[16,16]{0,1:T(8,128)(2,1)S(1)}, u32[]{:S(2)}, u32[]{:S(2)}) %collective-permute-start.2) | collective-permute-done | bytes 544 | tf_op jit(solution)/shard_map/while/body/eval_jaxpr/ppermute | solution.py:13
  183.3 6.0 %collective-permute-done.5 = bf16[16,16]{0,1:T(8,128)(2,1)S(1)} collective-permute-done((bf16[16,16]{0,1:T(8,128)(2,1)S(1)}, bf16[16,16]{0,1:T(8,128)(2,1)S(1)}, u32[]{:S(2)}, u32[]{:S(2)}) %collective-permute-start.5) | collective-permute-done | bytes 544 | tf_op jit(solution)/shard_map/ppermute | solution.py:13
  189.6 2.6 %fusion.13 = bf16[16,1024]{1,0:T(8,128)(2,1)} fusion(bf16[1024,1024]{1,0:T(8,128)(2,1)} %param.19, bf16[16,1024]{1,0:T(8,128)(2,1)S(1)} %copy-done.1, f32[16,1024]{1,0:T(8,128)S(1)} %div.36, bf16[16,1024]{1,0:T(8,128)(2,1)S(1)} %collective-permute-done.4), kind=kOutput, calls=%fused_computation.29 | convolution fusion | flops 33652736 | bytes 2260992 | tf_op jit(solution)/shard_map/dot_general | solution.py:117
  (375 shorter events, 38.8 us)
Async XLA Ops:
  1.6 23.8 %all-to-all-start.1 = ((s32[32,16,1]{0,2,1:T(1,128)}), s32[32,16,1]{0,2,1:T(1,128)S(1)}, u32[]{:S(2)}, u32[]{:S(2)}) async-start(s32[32,16,1]{0,2,1:T(1,128)} %copy.69), calls=%async_computation.1 | async-start | bytes 16384 | tf_op jit(solution)/shard_map/all_to_all | solution.py:72
  25.4 29.0 %all-to-all-start = ((bf16[16,32,1,1024]{3,1,2,0:T(8,128)(2,1)}), bf16[16,32,1,1024]{3,1,2,0:T(8,128)(2,1)}, u32[]{:S(2)}, u32[]{:S(2)}) async-start(bf16[16,32,1,1024]{3,1,2,0:T(8,128)(2,1)} %bitcast_dynamic-update-slice_fusion), calls=%async_computation | async-start | bytes 2097152 | tf_op jit(solution)/shard_map/all_to_all | solution.py:60
  64.8 8.5 %collective-permute-start.3 = (bf16[16,1024]{1,0:T(8,128)(2,1)S(1)}, bf16[16,1024]{1,0:T(8,128)(2,1)S(1)}, u32[]{:S(2)}, u32[]{:S(2)}) collective-permute-start(bf16[16,1024]{1,0:T(8,128)(2,1)S(1)} %convert_element_type.136), channel_id=1, source_target_pairs={{15,0},{0,1},{1,2},{2,3},{3,4},{4,5},{5,6},{6,7},{7,8},{8,9},{9,10... | collective-permute-start | bytes 98312 | tf_op jit(solution)/shard_map/while/body/eval_jaxpr/ppermute | solution.py:13
  65.5 7.8 %collective-permute-start = (bf16[16,1024]{1,0:T(8,128)(2,1)S(1)}, bf16[16,1024]{1,0:T(8,128)(2,1)S(1)}, u32[]{:S(2)}, u32[]{:S(2)}) collective-permute-start(bf16[16,1024]{1,0:T(8,128)(2,1)S(1)} %copy.150), channel_id=1, source_target_pairs={{15,0},{0,1},{1,2},{2,3},{3,4},{4,5},{5,6},{6,7},{7,8},{8,9},{9,10... | collective-permute-start | bytes 98312 | tf_op jit(solution)/shard_map/while/body/eval_jaxpr/ppermute | solution.py:13
  74.5 6.5 %collective-permute-start.3 = (bf16[16,1024]{1,0:T(8,128)(2,1)S(1)}, bf16[16,1024]{1,0:T(8,128)(2,1)S(1)}, u32[]{:S(2)}, u32[]{:S(2)}) collective-permute-start(bf16[16,1024]{1,0:T(8,128)(2,1)S(1)} %convert_element_type.136), channel_id=1, source_target_pairs={{15,0},{0,1},{1,2},{2,3},{3,4},{4,5},{5,6},{6,7},{7,8},{8,9},{9,10... | collective-permute-start | bytes 98312 | tf_op jit(solution)/shard_map/while/body/eval_jaxpr/ppermute | solution.py:13
  74.6 6.5 %collective-permute-start = (bf16[16,1024]{1,0:T(8,128)(2,1)S(1)}, bf16[16,1024]{1,0:T(8,128)(2,1)S(1)}, u32[]{:S(2)}, u32[]{:S(2)}) collective-permute-start(bf16[16,1024]{1,0:T(8,128)(2,1)S(1)} %copy.150), channel_id=1, source_target_pairs={{15,0},{0,1},{1,2},{2,3},{3,4},{4,5},{5,6},{6,7},{7,8},{8,9},{9,10... | collective-permute-start | bytes 98312 | tf_op jit(solution)/shard_map/while/body/eval_jaxpr/ppermute | solution.py:13
  82.3 6.5 %collective-permute-start.3 = (bf16[16,1024]{1,0:T(8,128)(2,1)S(1)}, bf16[16,1024]{1,0:T(8,128)(2,1)S(1)}, u32[]{:S(2)}, u32[]{:S(2)}) collective-permute-start(bf16[16,1024]{1,0:T(8,128)(2,1)S(1)} %convert_element_type.136), channel_id=1, source_target_pairs={{15,0},{0,1},{1,2},{2,3},{3,4},{4,5},{5,6},{6,7},{7,8},{8,9},{9,10... | collective-permute-start | bytes 98312 | tf_op jit(solution)/shard_map/while/body/eval_jaxpr/ppermute | solution.py:13
  82.4 6.5 %collective-permute-start = (bf16[16,1024]{1,0:T(8,128)(2,1)S(1)}, bf16[16,1024]{1,0:T(8,128)(2,1)S(1)}, u32[]{:S(2)}, u32[]{:S(2)}) collective-permute-start(bf16[16,1024]{1,0:T(8,128)(2,1)S(1)} %copy.150), channel_id=1, source_target_pairs={{15,0},{0,1},{1,2},{2,3},{3,4},{4,5},{5,6},{6,7},{7,8},{8,9},{9,10... | collective-permute-start | bytes 98312 | tf_op jit(solution)/shard_map/while/body/eval_jaxpr/ppermute | solution.py:13
  90.1 6.5 %collective-permute-start.3 = (bf16[16,1024]{1,0:T(8,128)(2,1)S(1)}, bf16[16,1024]{1,0:T(8,128)(2,1)S(1)}, u32[]{:S(2)}, u32[]{:S(2)}) collective-permute-start(bf16[16,1024]{1,0:T(8,128)(2,1)S(1)} %convert_element_type.136), channel_id=1, source_target_pairs={{15,0},{0,1},{1,2},{2,3},{3,4},{4,5},{5,6},{6,7},{7,8},{8,9},{9,10... | collective-permute-start | bytes 98312 | tf_op jit(solution)/shard_map/while/body/eval_jaxpr/ppermute | solution.py:13
  90.1 6.5 %collective-permute-start = (bf16[16,1024]{1,0:T(8,128)(2,1)S(1)}, bf16[16,1024]{1,0:T(8,128)(2,1)S(1)}, u32[]{:S(2)}, u32[]{:S(2)}) collective-permute-start(bf16[16,1024]{1,0:T(8,128)(2,1)S(1)} %copy.150), channel_id=1, source_target_pairs={{15,0},{0,1},{1,2},{2,3},{3,4},{4,5},{5,6},{6,7},{7,8},{8,9},{9,10... | collective-permute-start | bytes 98312 | tf_op jit(solution)/shard_map/while/body/eval_jaxpr/ppermute | solution.py:13
  97.8 6.5 %collective-permute-start.3 = (bf16[16,1024]{1,0:T(8,128)(2,1)S(1)}, bf16[16,1024]{1,0:T(8,128)(2,1)S(1)}, u32[]{:S(2)}, u32[]{:S(2)}) collective-permute-start(bf16[16,1024]{1,0:T(8,128)(2,1)S(1)} %convert_element_type.136), channel_id=1, source_target_pairs={{15,0},{0,1},{1,2},{2,3},{3,4},{4,5},{5,6},{6,7},{7,8},{8,9},{9,10... | collective-permute-start | bytes 98312 | tf_op jit(solution)/shard_map/while/body/eval_jaxpr/ppermute | solution.py:13
  97.9 6.5 %collective-permute-start = (bf16[16,1024]{1,0:T(8,128)(2,1)S(1)}, bf16[16,1024]{1,0:T(8,128)(2,1)S(1)}, u32[]{:S(2)}, u32[]{:S(2)}) collective-permute-start(bf16[16,1024]{1,0:T(8,128)(2,1)S(1)} %copy.150), channel_id=1, source_target_pairs={{15,0},{0,1},{1,2},{2,3},{3,4},{4,5},{5,6},{6,7},{7,8},{8,9},{9,10... | collective-permute-start | bytes 98312 | tf_op jit(solution)/shard_map/while/body/eval_jaxpr/ppermute | solution.py:13
  105.6 6.5 %collective-permute-start.3 = (bf16[16,1024]{1,0:T(8,128)(2,1)S(1)}, bf16[16,1024]{1,0:T(8,128)(2,1)S(1)}, u32[]{:S(2)}, u32[]{:S(2)}) collective-permute-start(bf16[16,1024]{1,0:T(8,128)(2,1)S(1)} %convert_element_type.136), channel_id=1, source_target_pairs={{15,0},{0,1},{1,2},{2,3},{3,4},{4,5},{5,6},{6,7},{7,8},{8,9},{9,10... | collective-permute-start | bytes 98312 | tf_op jit(solution)/shard_map/while/body/eval_jaxpr/ppermute | solution.py:13
  105.7 6.5 %collective-permute-start = (bf16[16,1024]{1,0:T(8,128)(2,1)S(1)}, bf16[16,1024]{1,0:T(8,128)(2,1)S(1)}, u32[]{:S(2)}, u32[]{:S(2)}) collective-permute-start(bf16[16,1024]{1,0:T(8,128)(2,1)S(1)} %copy.150), channel_id=1, source_target_pairs={{15,0},{0,1},{1,2},{2,3},{3,4},{4,5},{5,6},{6,7},{7,8},{8,9},{9,10... | collective-permute-start | bytes 98312 | tf_op jit(solution)/shard_map/while/body/eval_jaxpr/ppermute | solution.py:13
  113.4 6.5 %collective-permute-start.3 = (bf16[16,1024]{1,0:T(8,128)(2,1)S(1)}, bf16[16,1024]{1,0:T(8,128)(2,1)S(1)}, u32[]{:S(2)}, u32[]{:S(2)}) collective-permute-start(bf16[16,1024]{1,0:T(8,128)(2,1)S(1)} %convert_element_type.136), channel_id=1, source_target_pairs={{15,0},{0,1},{1,2},{2,3},{3,4},{4,5},{5,6},{6,7},{7,8},{8,9},{9,10... | collective-permute-start | bytes 98312 | tf_op jit(solution)/shard_map/while/body/eval_jaxpr/ppermute | solution.py:13
  113.4 6.5 %collective-permute-start = (bf16[16,1024]{1,0:T(8,128)(2,1)S(1)}, bf16[16,1024]{1,0:T(8,128)(2,1)S(1)}, u32[]{:S(2)}, u32[]{:S(2)}) collective-permute-start(bf16[16,1024]{1,0:T(8,128)(2,1)S(1)} %copy.150), channel_id=1, source_target_pairs={{15,0},{0,1},{1,2},{2,3},{3,4},{4,5},{5,6},{6,7},{7,8},{8,9},{9,10... | collective-permute-start | bytes 98312 | tf_op jit(solution)/shard_map/while/body/eval_jaxpr/ppermute | solution.py:13
  121.1 6.5 %collective-permute-start.3 = (bf16[16,1024]{1,0:T(8,128)(2,1)S(1)}, bf16[16,1024]{1,0:T(8,128)(2,1)S(1)}, u32[]{:S(2)}, u32[]{:S(2)}) collective-permute-start(bf16[16,1024]{1,0:T(8,128)(2,1)S(1)} %convert_element_type.136), channel_id=1, source_target_pairs={{15,0},{0,1},{1,2},{2,3},{3,4},{4,5},{5,6},{6,7},{7,8},{8,9},{9,10... | collective-permute-start | bytes 98312 | tf_op jit(solution)/shard_map/while/body/eval_jaxpr/ppermute | solution.py:13
  121.2 6.5 %collective-permute-start = (bf16[16,1024]{1,0:T(8,128)(2,1)S(1)}, bf16[16,1024]{1,0:T(8,128)(2,1)S(1)}, u32[]{:S(2)}, u32[]{:S(2)}) collective-permute-start(bf16[16,1024]{1,0:T(8,128)(2,1)S(1)} %copy.150), channel_id=1, source_target_pairs={{15,0},{0,1},{1,2},{2,3},{3,4},{4,5},{5,6},{6,7},{7,8},{8,9},{9,10... | collective-permute-start | bytes 98312 | tf_op jit(solution)/shard_map/while/body/eval_jaxpr/ppermute | solution.py:13
  128.9 6.5 %collective-permute-start.3 = (bf16[16,1024]{1,0:T(8,128)(2,1)S(1)}, bf16[16,1024]{1,0:T(8,128)(2,1)S(1)}, u32[]{:S(2)}, u32[]{:S(2)}) collective-permute-start(bf16[16,1024]{1,0:T(8,128)(2,1)S(1)} %convert_element_type.136), channel_id=1, source_target_pairs={{15,0},{0,1},{1,2},{2,3},{3,4},{4,5},{5,6},{6,7},{7,8},{8,9},{9,10... | collective-permute-start | bytes 98312 | tf_op jit(solution)/shard_map/while/body/eval_jaxpr/ppermute | solution.py:13
  128.9 6.5 %collective-permute-start = (bf16[16,1024]{1,0:T(8,128)(2,1)S(1)}, bf16[16,1024]{1,0:T(8,128)(2,1)S(1)}, u32[]{:S(2)}, u32[]{:S(2)}) collective-permute-start(bf16[16,1024]{1,0:T(8,128)(2,1)S(1)} %copy.150), channel_id=1, source_target_pairs={{15,0},{0,1},{1,2},{2,3},{3,4},{4,5},{5,6},{6,7},{7,8},{8,9},{9,10... | collective-permute-start | bytes 98312 | tf_op jit(solution)/shard_map/while/body/eval_jaxpr/ppermute | solution.py:13
  136.6 6.5 %collective-permute-start.3 = (bf16[16,1024]{1,0:T(8,128)(2,1)S(1)}, bf16[16,1024]{1,0:T(8,128)(2,1)S(1)}, u32[]{:S(2)}, u32[]{:S(2)}) collective-permute-start(bf16[16,1024]{1,0:T(8,128)(2,1)S(1)} %convert_element_type.136), channel_id=1, source_target_pairs={{15,0},{0,1},{1,2},{2,3},{3,4},{4,5},{5,6},{6,7},{7,8},{8,9},{9,10... | collective-permute-start | bytes 98312 | tf_op jit(solution)/shard_map/while/body/eval_jaxpr/ppermute | solution.py:13
  136.7 6.5 %collective-permute-start = (bf16[16,1024]{1,0:T(8,128)(2,1)S(1)}, bf16[16,1024]{1,0:T(8,128)(2,1)S(1)}, u32[]{:S(2)}, u32[]{:S(2)}) collective-permute-start(bf16[16,1024]{1,0:T(8,128)(2,1)S(1)} %copy.150), channel_id=1, source_target_pairs={{15,0},{0,1},{1,2},{2,3},{3,4},{4,5},{5,6},{6,7},{7,8},{8,9},{9,10... | collective-permute-start | bytes 98312 | tf_op jit(solution)/shard_map/while/body/eval_jaxpr/ppermute | solution.py:13
  144.4 6.5 %collective-permute-start.3 = (bf16[16,1024]{1,0:T(8,128)(2,1)S(1)}, bf16[16,1024]{1,0:T(8,128)(2,1)S(1)}, u32[]{:S(2)}, u32[]{:S(2)}) collective-permute-start(bf16[16,1024]{1,0:T(8,128)(2,1)S(1)} %convert_element_type.136), channel_id=1, source_target_pairs={{15,0},{0,1},{1,2},{2,3},{3,4},{4,5},{5,6},{6,7},{7,8},{8,9},{9,10... | collective-permute-start | bytes 98312 | tf_op jit(solution)/shard_map/while/body/eval_jaxpr/ppermute | solution.py:13
  144.5 6.5 %collective-permute-start = (bf16[16,1024]{1,0:T(8,128)(2,1)S(1)}, bf16[16,1024]{1,0:T(8,128)(2,1)S(1)}, u32[]{:S(2)}, u32[]{:S(2)}) collective-permute-start(bf16[16,1024]{1,0:T(8,128)(2,1)S(1)} %copy.150), channel_id=1, source_target_pairs={{15,0},{0,1},{1,2},{2,3},{3,4},{4,5},{5,6},{6,7},{7,8},{8,9},{9,10... | collective-permute-start | bytes 98312 | tf_op jit(solution)/shard_map/while/body/eval_jaxpr/ppermute | solution.py:13
  152.2 6.5 %collective-permute-start.3 = (bf16[16,1024]{1,0:T(8,128)(2,1)S(1)}, bf16[16,1024]{1,0:T(8,128)(2,1)S(1)}, u32[]{:S(2)}, u32[]{:S(2)}) collective-permute-start(bf16[16,1024]{1,0:T(8,128)(2,1)S(1)} %convert_element_type.136), channel_id=1, source_target_pairs={{15,0},{0,1},{1,2},{2,3},{3,4},{4,5},{5,6},{6,7},{7,8},{8,9},{9,10... | collective-permute-start | bytes 98312 | tf_op jit(solution)/shard_map/while/body/eval_jaxpr/ppermute | solution.py:13
  152.2 6.5 %collective-permute-start = (bf16[16,1024]{1,0:T(8,128)(2,1)S(1)}, bf16[16,1024]{1,0:T(8,128)(2,1)S(1)}, u32[]{:S(2)}, u32[]{:S(2)}) collective-permute-start(bf16[16,1024]{1,0:T(8,128)(2,1)S(1)} %copy.150), channel_id=1, source_target_pairs={{15,0},{0,1},{1,2},{2,3},{3,4},{4,5},{5,6},{6,7},{7,8},{8,9},{9,10... | collective-permute-start | bytes 98312 | tf_op jit(solution)/shard_map/while/body/eval_jaxpr/ppermute | solution.py:13
  159.9 6.5 %collective-permute-start.3 = (bf16[16,1024]{1,0:T(8,128)(2,1)S(1)}, bf16[16,1024]{1,0:T(8,128)(2,1)S(1)}, u32[]{:S(2)}, u32[]{:S(2)}) collective-permute-start(bf16[16,1024]{1,0:T(8,128)(2,1)S(1)} %convert_element_type.136), channel_id=1, source_target_pairs={{15,0},{0,1},{1,2},{2,3},{3,4},{4,5},{5,6},{6,7},{7,8},{8,9},{9,10... | collective-permute-start | bytes 98312 | tf_op jit(solution)/shard_map/while/body/eval_jaxpr/ppermute | solution.py:13
  160.0 6.5 %collective-permute-start = (bf16[16,1024]{1,0:T(8,128)(2,1)S(1)}, bf16[16,1024]{1,0:T(8,128)(2,1)S(1)}, u32[]{:S(2)}, u32[]{:S(2)}) collective-permute-start(bf16[16,1024]{1,0:T(8,128)(2,1)S(1)} %copy.150), channel_id=1, source_target_pairs={{15,0},{0,1},{1,2},{2,3},{3,4},{4,5},{5,6},{6,7},{7,8},{8,9},{9,10... | collective-permute-start | bytes 98312 | tf_op jit(solution)/shard_map/while/body/eval_jaxpr/ppermute | solution.py:13
  167.7 6.5 %collective-permute-start.3 = (bf16[16,1024]{1,0:T(8,128)(2,1)S(1)}, bf16[16,1024]{1,0:T(8,128)(2,1)S(1)}, u32[]{:S(2)}, u32[]{:S(2)}) collective-permute-start(bf16[16,1024]{1,0:T(8,128)(2,1)S(1)} %convert_element_type.136), channel_id=1, source_target_pairs={{15,0},{0,1},{1,2},{2,3},{3,4},{4,5},{5,6},{6,7},{7,8},{8,9},{9,10... | collective-permute-start | bytes 98312 | tf_op jit(solution)/shard_map/while/body/eval_jaxpr/ppermute | solution.py:13
  167.8 6.5 %collective-permute-start = (bf16[16,1024]{1,0:T(8,128)(2,1)S(1)}, bf16[16,1024]{1,0:T(8,128)(2,1)S(1)}, u32[]{:S(2)}, u32[]{:S(2)}) collective-permute-start(bf16[16,1024]{1,0:T(8,128)(2,1)S(1)} %copy.150), channel_id=1, source_target_pairs={{15,0},{0,1},{1,2},{2,3},{3,4},{4,5},{5,6},{6,7},{7,8},{8,9},{9,10... | collective-permute-start | bytes 98312 | tf_op jit(solution)/shard_map/while/body/eval_jaxpr/ppermute | solution.py:13
  175.5 6.5 %collective-permute-start.3 = (bf16[16,1024]{1,0:T(8,128)(2,1)S(1)}, bf16[16,1024]{1,0:T(8,128)(2,1)S(1)}, u32[]{:S(2)}, u32[]{:S(2)}) collective-permute-start(bf16[16,1024]{1,0:T(8,128)(2,1)S(1)} %convert_element_type.136), channel_id=1, source_target_pairs={{15,0},{0,1},{1,2},{2,3},{3,4},{4,5},{5,6},{6,7},{7,8},{8,9},{9,10... | collective-permute-start | bytes 98312 | tf_op jit(solution)/shard_map/while/body/eval_jaxpr/ppermute | solution.py:13
  175.5 6.5 %collective-permute-start = (bf16[16,1024]{1,0:T(8,128)(2,1)S(1)}, bf16[16,1024]{1,0:T(8,128)(2,1)S(1)}, u32[]{:S(2)}, u32[]{:S(2)}) collective-permute-start(bf16[16,1024]{1,0:T(8,128)(2,1)S(1)} %copy.150), channel_id=1, source_target_pairs={{15,0},{0,1},{1,2},{2,3},{3,4},{4,5},{5,6},{6,7},{7,8},{8,9},{9,10... | collective-permute-start | bytes 98312 | tf_op jit(solution)/shard_map/while/body/eval_jaxpr/ppermute | solution.py:13
  (37 other events, 302.4 us)
